TPU v7x, 128 devices: a whole 4x4x4 slice. The times are simulated.
128 devices in a mesh: dp: 32 (over x, z_hi, y), tensor: 4 (over z_lo, core).
Axes of the slice: x: 4, y: 4, z: 4 (z_hi: 2, z_lo: 2; z = z_hi * 2 + z_lo), core: 2. Of those that a mesh axis runs over, the one named last changes fastest.
Arguments:
- tokens: bfloat16 [65536, 1024], P(('dp', 'tensor')), may hold values from -16 to 16
- prompts: bfloat16 [32, 64, 1024], P('dp'), may hold values from -6 to 6
- w_attn: bfloat16 [3, 1024, 1024], P(None, None, 'tensor'), may hold values from -0.1875 to 0.1875
- w_out: bfloat16 [1024, 1024], P('tensor'), may hold values from -0.1875 to 0.1875
- norm_gain: float32 [2, 1024], replicated, may hold values from 0.1 to 1.9
- norm_bias: float32 [2, 1024], replicated, may hold values from -3 to 3
- w_in: bfloat16 [1024, 4096], P(None, 'tensor'), may hold values from -0.1875 to 0.1875
- b_in: float32 [4096], P('tensor'), may hold values from -3 to 3
- w_down: bfloat16 [4096, 1024], P('tensor'), may hold values from -0.09375 to 0.09375
- index_rows: bfloat16 [65536, 1024], P('dp'), may hold values from -6 to 6
- lengths: int32 [32, 32], P('dp'), may hold values from 1 to 512, 2048 in all within a row
- groups: int32 [1024], P('dp'), may hold values from 0 to 31
- candidates: int32 [1024, 64], P(('dp', 'tensor')), may hold values from 0 to 65535
Outputs:
- scores: float32 [1024, 64], P(('dp', 'tensor'))
All inputs are finite; a program needn't handle non-finite values.
Results may differ from a plain program's by a relative error of at most 0.01.
Values may be sent and summed in bfloat16 or wider, within the bound.
No kernel may reach another device: no remote copies, remote signals or barrier semaphores. Data moves between devices by JAX's collectives and lax.ppermute only.
A program may use at most 128 MiB of HBM per device.

v0:
```python
import jax
import jax.numpy as jnp
from jax import lax
from jax.sharding import PartitionSpec as P

D = 1024
HEAD_DIM = 64


def layer_norm(values, gain, bias):
    mean = jnp.mean(values, axis=-1, keepdims=True)
    centred = values - mean
    var = jnp.mean(centred * centred, axis=-1, keepdims=True)
    return centred * lax.rsqrt(var + 1e-05) * gain + bias


def project(block, weight):
    return jnp.dot(block, weight, preferred_element_type=jnp.float32).astype(jnp.bfloat16)


def shards(
    tokens,
    prompts,
    w_attn,
    w_out,
    norm_gain,
    norm_bias,
    w_in,
    b_in,
    w_down,
    index_rows,
    lengths,
    groups,
    candidates,
):
    shard_rows = tokens.shape[0]
    tok_dev = shard_rows * lax.axis_size("tensor")
    columns = w_attn.shape[2]
    heads_here = columns // HEAD_DIM
    scale = HEAD_DIM ** (-0.5)
    whole = lax.all_gather(tokens, "tensor", axis=0, tiled=True)
    query = (jnp.dot(whole, w_attn[0], preferred_element_type=jnp.float32) * scale).astype(
        jnp.bfloat16
    )
    keys = project(whole, w_attn[1])
    values = project(whole, w_attn[2])
    every_prompt = lax.all_gather(prompts, "dp", axis=0, tiled=True)
    flat = every_prompt.reshape(-1, every_prompt.shape[2])
    prompt_key = project(flat, w_attn[1])
    prompt_value = project(flat, w_attn[2])
    prompt_len = prompts.shape[1]
    prompt_rows = prompt_key.shape[0]
    lens = lengths[0]
    texts_here = lens.shape[0]
    text_ids = jnp.arange(texts_here, dtype=jnp.int32)
    ends = jnp.cumsum(lens)
    position = jnp.arange(tok_dev, dtype=jnp.int32)
    seg = jnp.sum((position[:, None] >= ends[None, :]).astype(jnp.int32), axis=1)
    tok_group = jnp.sum(jnp.where(seg[:, None] == text_ids[None, :], groups[None, :], 0), axis=1)
    key_group = jnp.arange(prompt_rows, dtype=jnp.int32) // prompt_len
    all_keys = jnp.concatenate([keys, prompt_key], axis=0).reshape(-1, heads_here, HEAD_DIM)
    all_values = jnp.concatenate([values, prompt_value], axis=0).reshape(-1, heads_here, HEAD_DIM)
    block = min(512, tok_dev)

    def attend(number):
        start = number * block
        q_block = lax.dynamic_slice_in_dim(query, start, block, 0).reshape(
            block, heads_here, HEAD_DIM
        )
        seg_block = lax.dynamic_slice_in_dim(seg, start, block, 0)
        group_block = lax.dynamic_slice_in_dim(tok_group, start, block, 0)
        allowed = jnp.concatenate(
            [seg_block[:, None] == seg[None, :], group_block[:, None] == key_group[None, :]], axis=1
        )
        logits = jnp.einsum("qhe,khe->hqk", q_block, all_keys, preferred_element_type=jnp.float32)
        logits = jnp.where(allowed[None], logits, jnp.float32(-1e30))
        top = jnp.max(logits, axis=2, keepdims=True)
        weights = jnp.exp(logits - top)
        total = jnp.sum(weights, axis=2, keepdims=True)
        probs = (weights / total).astype(jnp.bfloat16)
        mixed = jnp.einsum("hqk,khe->qhe", probs, all_values, preferred_element_type=jnp.float32)
        return mixed.astype(jnp.bfloat16).reshape(block, columns)

    context = lax.map(attend, jnp.arange(tok_dev // block, dtype=jnp.int32)).reshape(
        tok_dev, columns
    )
    my_start = lax.axis_index("tensor") * shard_rows
    attn_part = lax.psum_scatter(
        jnp.dot(context, w_out, preferred_element_type=jnp.float32),
        "tensor",
        scatter_dimension=0,
        tiled=True,
    )
    normed_rows = layer_norm(
        tokens.astype(jnp.float32) + attn_part, norm_gain[0], norm_bias[0]
    ).astype(jnp.bfloat16)
    expanded = jax.nn.gelu(
        jnp.dot(
            lax.all_gather(normed_rows, "tensor", axis=0, tiled=True),
            w_in,
            preferred_element_type=jnp.float32,
        )
        + b_in,
        approximate=False,
    ).astype(jnp.bfloat16)
    reduced = lax.psum_scatter(
        jnp.dot(expanded, w_down, preferred_element_type=jnp.float32).astype(jnp.bfloat16),
        "tensor",
        scatter_dimension=0,
        tiled=True,
    ).astype(jnp.float32)
    output = layer_norm(
        normed_rows.astype(jnp.float32) + reduced, norm_gain[1], norm_bias[1]
    ).astype(jnp.bfloat16)
    seg_rows = lax.dynamic_slice_in_dim(seg, my_start, shard_rows, 0)
    member = (text_ids[:, None] == seg_rows[None, :]).astype(jnp.bfloat16)
    partial_sums = jnp.dot(member, output, preferred_element_type=jnp.float32)
    pooled_sums = lax.psum_scatter(partial_sums, "tensor", scatter_dimension=0, tiled=True)
    mine = pooled_sums.shape[0]
    my_lens = lax.dynamic_slice_in_dim(lens, lax.axis_index("tensor") * mine, mine, 0)
    pooled = pooled_sums / my_lens[:, None].astype(jnp.float32)
    square = jnp.mean(pooled * pooled, axis=1, keepdims=True)
    embedding = (pooled * lax.rsqrt(square + 1e-06)).astype(jnp.bfloat16)
    asked_vectors, asked_rows = (
        lax.all_gather(embedding, "dp", axis=0, tiled=True),
        lax.all_gather(candidates, "dp", axis=0, tiled=True),
    )
    held = index_rows.shape[0]
    local_rows = asked_rows - lax.axis_index("dp") * held
    owned = (local_rows >= 0) & (local_rows < held)
    table = jnp.dot(asked_vectors, index_rows.T, preferred_element_type=jnp.float32) * D ** (-0.5)
    picked = jnp.take_along_axis(table, jnp.clip(local_rows, 0, held - 1), axis=1)
    picked = jnp.where(owned, picked, jnp.float32(0.0))
    return lax.psum_scatter(
        picked.astype(jnp.bfloat16), "dp", scatter_dimension=0, tiled=True
    ).astype(jnp.float32)


def solution(mesh):
    placed = (
        P(("dp", "tensor"), None),
        P("dp", None, None),
        P(None, None, "tensor"),
        P("tensor", None),
        P(),
        P(),
        P(None, "tensor"),
        P("tensor"),
        P("tensor", None),
        P("dp", None),
        P("dp", None),
        P("dp"),
        P(("dp", "tensor"), None),
    )
    return jax.shard_map(
        shards, mesh=mesh, in_specs=placed, out_specs=P(("dp", "tensor"), None), check_vma=False
    )
```

profile of v0, /device:TPU:0, one launch (start us, length us, event | category | flops | bytes accessed | tf_op | source)
XLA Modules:
  0.0 1021.1 jit_solution(8762261364968548644)
XLA Ops:
  6.5 0.7 all-gather.4.cloned.1.call-update
  7.3 0.7 all-gather.6.cloned.1.call-update
  8.1 0.7 copy.28
  9.1 0.8 select_reduce_fusion.1
  9.9 47.5 %all-gather.4.cloned.1.call-done = bf16[2048,1024]{1,0:T(8,128)(2,1)} async-done(((bf16[512,1024]{1,0:T(8,128)(2,1)}), bf16[2048,1024]{1,0:T(8,128)(2,1)}) %all-gather.4.cloned.1.call-update) | async-done | bytes 4194320 | tf_op jit(solution)/shard_map/all_gather | solution.py:41
  57.4 3.7 convolution_convert_fusion.1
  61.5 2.3 convolution_convert_fusion.3
  63.7 2.3 fusion.48
  66.1 78.2 %all-gather.6.cloned.1.call-done = bf16[32,64,1024]{2,1,0:T(8,128)(2,1)} async-done(((bf16[1,64,1024]{2,1,0:T(8,128)(2,1)}), bf16[32,64,1024]{2,1,0:T(8,128)(2,1)}) %all-gather.6.cloned.1.call-update) | async-done | bytes 4194320 | tf_op jit(solution)/shard_map/all_gather | solution.py:47
  144.3 4.7 convolution_convert_fusion
  149.0 2.4 convolution_convert_fusion.2
  151.4 1.4 pad_maximum_fusion
  152.9 4.1 copy.29
  157.0 2.7 pad_maximum_fusion.1
  159.7 4.1 copy.30
  163.8 158.4 %while.11 = (s32[]{:T(128)}, bf16[4,512,256]{2,1,0:T(8,128)(2,1)}, s32[4]{0:T(128)S(1)}, s32[2048]{0:T(1024)S(1)}, s32[2048]{0:T(1024)S(1)}, /*index=5*/bf16[204...) while((s32[]{:T(128)}, bf16[4,512,256]{2,1,0:T(8,128)(2,1)}, ...), condition=%wide.region_6.7_spmd.clone, body=%wide.region_3.6_spmd.clone.sunk | while | flops 3284297728 | bytes 19714248 | solution.py:84
  164.1 0.7 dynamic_slice.32
  165.7 1.0 constant_dynamic-slice_fusion.2
  166.8 1.3 broadcast_compare_fusion.3
  168.1 1.4 pad_add_fusion.2
  169.6 14.5 %fusion.133 = f32[4,512]{1,0:T(4,128)S(1)} fusion(pred[512,4096]{1,0:T(8,128)(4,1)} %pad_add_fusion.2, bf16[512,4,64]{0,2,1:T(8,128)(2,1)S(1)} %bitcast.71, bf16[4096,4,64]{0,2,1:T(8,128)(2,1)} %get-tuple-element.208), kind=kOutput, calls=%fused_computation.127.clone.1 | convolution fusion | flops 1098911744 | bytes 4464640 | tf_op jit(solution)/shard_map/while/body/eval_jaxpr/sub | solution.py:78
  184.0 16.2 %fusion.134 = bf16[4,512,64]{1,2,0:T(8,128)(2,1)S(1)} fusion(bf16[4096,4,64]{0,2,1:T(8,128)(2,1)} %get-tuple-element.209, f32[4,512]{1,0:T(4,128)S(1)} %fusion.133, pred[512,4096]{1,0:T(8,128)(4,1)} %pad_add_fusion.2, bf16[512,4,64]{0,2,1:T(8,128)(2,1)S(1)} %bitcast.72, bf16[4096,4,64]{0,2,1:T(8,128)(2,1)} %get-tuple-element.208), kind=kOutput, calls=%fused_computation.14.clone.1 | convolution fusion | flops 2181175296 | bytes 6823936 | tf_op jit(solution)/shard_map/while/body/eval_jaxpr/hqk,khe->qhe/dot_general | solution.py:81
  200.4 0.7 constant_dynamic-update-slice_fusion.2
  201.1 0.7 dynamic_slice.32
  202.6 1.0 constant_dynamic-slice_fusion.2
  203.8 1.3 broadcast_compare_fusion.3
  205.1 1.4 pad_add_fusion.2
  206.5 14.5 %fusion.133 = f32[4,512]{1,0:T(4,128)S(1)} fusion(pred[512,4096]{1,0:T(8,128)(4,1)} %pad_add_fusion.2, bf16[512,4,64]{0,2,1:T(8,128)(2,1)S(1)} %bitcast.71, bf16[4096,4,64]{0,2,1:T(8,128)(2,1)} %get-tuple-element.208), kind=kOutput, calls=%fused_computation.127.clone.1 | convolution fusion | flops 1098911744 | bytes 4464640 | tf_op jit(solution)/shard_map/while/body/eval_jaxpr/sub | solution.py:78
  221.0 16.2 %fusion.134 = bf16[4,512,64]{1,2,0:T(8,128)(2,1)S(1)} fusion(bf16[4096,4,64]{0,2,1:T(8,128)(2,1)} %get-tuple-element.209, f32[4,512]{1,0:T(4,128)S(1)} %fusion.133, pred[512,4096]{1,0:T(8,128)(4,1)} %pad_add_fusion.2, bf16[512,4,64]{0,2,1:T(8,128)(2,1)S(1)} %bitcast.72, bf16[4096,4,64]{0,2,1:T(8,128)(2,1)} %get-tuple-element.208), kind=kOutput, calls=%fused_computation.14.clone.1 | convolution fusion | flops 2181175296 | bytes 6823936 | tf_op jit(solution)/shard_map/while/body/eval_jaxpr/hqk,khe->qhe/dot_general | solution.py:81
  237.4 0.7 constant_dynamic-update-slice_fusion.2
  238.1 0.7 dynamic_slice.32
  239.6 1.0 constant_dynamic-slice_fusion.2
  240.7 1.3 broadcast_compare_fusion.3
  242.1 1.4 pad_add_fusion.2
  243.5 14.5 %fusion.133 = f32[4,512]{1,0:T(4,128)S(1)} fusion(pred[512,4096]{1,0:T(8,128)(4,1)} %pad_add_fusion.2, bf16[512,4,64]{0,2,1:T(8,128)(2,1)S(1)} %bitcast.71, bf16[4096,4,64]{0,2,1:T(8,128)(2,1)} %get-tuple-element.208), kind=kOutput, calls=%fused_computation.127.clone.1 | convolution fusion | flops 1098911744 | bytes 4464640 | tf_op jit(solution)/shard_map/while/body/eval_jaxpr/sub | solution.py:78
  258.0 16.2 %fusion.134 = bf16[4,512,64]{1,2,0:T(8,128)(2,1)S(1)} fusion(bf16[4096,4,64]{0,2,1:T(8,128)(2,1)} %get-tuple-element.209, f32[4,512]{1,0:T(4,128)S(1)} %fusion.133, pred[512,4096]{1,0:T(8,128)(4,1)} %pad_add_fusion.2, bf16[512,4,64]{0,2,1:T(8,128)(2,1)S(1)} %bitcast.72, bf16[4096,4,64]{0,2,1:T(8,128)(2,1)} %get-tuple-element.208), kind=kOutput, calls=%fused_computation.14.clone.1 | convolution fusion | flops 2181175296 | bytes 6823936 | tf_op jit(solution)/shard_map/while/body/eval_jaxpr/hqk,khe->qhe/dot_general | solution.py:81
  274.3 0.7 constant_dynamic-update-slice_fusion.2
  275.1 0.7 dynamic_slice.32
  276.6 1.0 constant_dynamic-slice_fusion.2
  277.7 1.3 broadcast_compare_fusion.3
  279.1 1.4 pad_add_fusion.2
  280.5 14.5 %fusion.133 = f32[4,512]{1,0:T(4,128)S(1)} fusion(pred[512,4096]{1,0:T(8,128)(4,1)} %pad_add_fusion.2, bf16[512,4,64]{0,2,1:T(8,128)(2,1)S(1)} %bitcast.71, bf16[4096,4,64]{0,2,1:T(8,128)(2,1)} %get-tuple-element.208), kind=kOutput, calls=%fused_computation.127.clone.1 | convolution fusion | flops 1098911744 | bytes 4464640 | tf_op jit(solution)/shard_map/while/body/eval_jaxpr/sub | solution.py:78
  295.0 16.2 %fusion.134 = bf16[4,512,64]{1,2,0:T(8,128)(2,1)S(1)} fusion(bf16[4096,4,64]{0,2,1:T(8,128)(2,1)} %get-tuple-element.209, f32[4,512]{1,0:T(4,128)S(1)} %fusion.133, pred[512,4096]{1,0:T(8,128)(4,1)} %pad_add_fusion.2, bf16[512,4,64]{0,2,1:T(8,128)(2,1)S(1)} %bitcast.72, bf16[4096,4,64]{0,2,1:T(8,128)(2,1)} %get-tuple-element.208), kind=kOutput, calls=%fused_computation.14.clone.1 | convolution fusion | flops 2181175296 | bytes 6823936 | tf_op jit(solution)/shard_map/while/body/eval_jaxpr/hqk,khe->qhe/dot_general | solution.py:81
  311.3 0.7 constant_dynamic-update-slice_fusion.2
  322.1 5.8 fusion.97
  328.1 0.6 copy-done.6
  328.7 75.2 %reduce-scatter.4.cloned.1.call-done = f32[512,1024]{1,0:T(8,128)} async-done(((f32[2048,1024]{1,0:T(8,128)}), f32[512,1024]{1,0:T(8,128)}) %reduce-scatter.4.cloned.1.call-update) | async-done | bytes 2097168 | tf_op jit(solution)/shard_map/reduce_scatter | solution.py:88
  403.9 2.0 fusion.52
  406.6 1.6 add_convert_fusion.1
  408.3 46.9 %all-gather.8.cloned.1.call-done = bf16[2048,1024]{1,0:T(8,128)(2,1)} async-done(((bf16[512,1024]{1,0:T(8,128)(2,1)}), bf16[2048,1024]{1,0:T(8,128)(2,1)}) %all-gather.8.cloned.1.call-update) | async-done | bytes 4194320 | tf_op jit(solution)/shard_map/all_gather | solution.py:99
  455.3 28.5 %fusion.43 = bf16[2048,1024]{1,0:T(8,128)(2,1)} fusion(bf16[1024,1024]{1,0:T(8,128)(2,1)S(1)} %copy-done, f32[1024]{0:T(1024)S(1)} %copy-done.13, bf16[2048,1024]{1,0:T(8,128)(2,1)} %all-gather.8.cloned.1.call-done, bf16[1024,1024]{1,0:T(8,128)(2,1)} %param.21), kind=kOutput, calls=%fused_computation.47 | convolution fusion | flops 8730443776 | bytes 12587008 | tf_op jit(solution)/shard_map/dot_general | solution.py:107
  484.5 95.9 %all_gather.15 = s32[256,64]{1,0:T(8,128)S(1)} all-gather(s32[8,64]{1,0:T(8,128)S(1)} %copy-done.8), channel_id=1, replica_groups=mesh['dp'=32,'tensor'=4] {'dp'}, dimensions={0}, use_global_device_ids=true | all-gather | bytes 67584 | tf_op jit(solution)/shard_map/all_gather | solution.py:126
  580.4 1.7 fusion.50
  582.1 1.7 multiply_reduce_fusion
  583.8 1.3 fusion.51
  585.4 0.6 dynamic-slice.1
  586.7 9.1 reduce-scatter.8.cloned.1.call-done
  595.8 0.9 multiply_reduce_fusion.2
  596.7 0.8 multiply_convert_fusion
  597.6 97.2 %all_gather.19 = bf16[256,1024]{1,0:T(8,128)(2,1)S(1)} all-gather(bf16[8,1024]{1,0:T(8,128)(2,1)S(1)} %multiply_convert_fusion), channel_id=1, replica_groups=mesh['dp'=32,'tensor'=4] {'dp'}, dimensions={0}, use_global_device_ids=true | all-gather | bytes 540672 | tf_op jit(solution)/shard_map/all_gather | solution.py:125
  694.8 3.5 convolution_multiply_fusion
  698.2 138.8 %gather_fusion = bf16[16384]{0:T(1024)(128)(2,1)S(1)} fusion(bf16[256,2048]{1,0:T(8,128)(2,1)S(1)} %convolution_multiply_fusion, s32[16384]{0:T(1024)S(1)} %reshape.112), kind=kCustom, calls=%fused_computation | custom fusion | bytes 196608 | tf_op jit(solution)/shard_map/jit(take_along_axis)/gather | solution.py:132
  837.3 176.2 %all-reduce = bf16[256,64]{1,0:T(8,128)(2,1)S(1)} all-reduce(bf16[256,64]{1,0:T(8,128)(2,1)S(1)} %select_convert_fusion), channel_id=5, replica_groups=mesh['dp'=32,'tensor'=4] {'dp'}, use_global_device_ids=true, to_apply=%region_15.16.clone | all-reduce | flops 16384 | bytes 65536
  1013.5 0.6 dynamic-slice_convert_fusion
  (79 shorter events, 4.4 us)
Async XLA Ops:
  6.5 448.7 %copy-start = (bf16[1024,1024]{1,0:T(8,128)(2,1)S(1)}, bf16[1024,1024]{1,0:T(8,128)(2,1)}, u32[]{:S(2)}) copy-start(bf16[1024,1024]{1,0:T(8,128)(2,1)} %param.23) | copy-start | bytes 6291460
  6.5 50.9 %all-gather.4.cloned.1.call-start = ((), (), s32[]{:S(2)}) async-start(), calls=%async_computation.3 | async-start | bytes 5242880 | tf_op jit(solution)/shard_map/all_gather | solution.py:41
  7.3 137.0 %all-gather.6.cloned.1.call-start = ((), (), s32[]{:S(2)}) async-start(), calls=%async_computation.4 | async-start | bytes 4325376 | tf_op jit(solution)/shard_map/all_gather | solution.py:47
  8.0 395.9 %reduce-scatter.4.cloned.1.call-start = ((), (), s32[]{:S(2)}) async-start(), calls=%async_computation.5 | async-start | bytes 10485760 | tf_op jit(solution)/shard_map/reduce_scatter | solution.py:88
  57.4 3.7 copy-start.10
  57.4 4.1 copy-start.12
  144.3 4.7 copy-start.11
  149.0 2.4 copy-start.5
  328.0 0.7 copy-start.6
  328.0 0.7 copy-start.7
  328.0 75.9 %copy-start.3 = (bf16[512,1024]{1,0:T(8,128)(2,1)S(1)}, bf16[512,1024]{1,0:T(8,128)(2,1)}, u32[]{:S(2)}) copy-start(bf16[512,1024]{1,0:T(8,128)(2,1)} %param.15) | copy-start | bytes 3145732
  328.0 127.2 %all-gather.8.cloned.1.call-start = ((), (), s32[]{:S(2)}) async-start(), calls=%async_computation.6 | async-start | bytes 5242880 | tf_op jit(solution)/shard_map/all_gather | solution.py:99
  403.9 2.2 copy-start.1
  406.2 49.1 %copy-start.13 = (f32[1024]{0:T(1024)S(1)}, f32[1024]{0:T(1024)}, u32[]{:S(2)}) copy-start(f32[1024]{0:T(1024)} %param.22) | copy-start | bytes 12292
  408.3 172.1 %reduce-scatter.6.cloned.1.call-start = ((), (), s32[]{:S(2)}) async-start(), calls=%async_computation.7 | async-start | bytes 5242880 | tf_op jit(solution)/shard_map/reduce_scatter | solution.py:106
  483.8 0.7 copy-start.8
  483.8 96.6 %copy-start.2 = (bf16[512,1024]{1,0:T(8,128)(2,1)S(1)}, bf16[512,1024]{1,0:T(8,128)(2,1)}, u32[]{:S(2)}) copy-start(bf16[512,1024]{1,0:T(8,128)(2,1)} %add_convert_fusion.1) | copy-start | bytes 3145732
  483.8 112.0 %reduce-scatter.8.cloned.1.call-start = ((), (), s32[]{:S(2)}) async-start(), calls=%async_computation.8 | async-start | bytes 163840 | tf_op jit(solution)/shard_map/reduce_scatter | solution.py:118
  580.4 5.0 copy-start.14
  580.4 6.2 copy-start.9
  580.4 3.4 copy-start.4
Sparse Core Ops, SparseCore 0:
  9.0 48.3 all-gather.3
  60.5 83.7 all-gather.5
  328.1 75.7 reduce-scatter.3
  408.4 46.8 all-gather.7
  483.9 47.6 reduce-scatter.5
  585.3 10.4 reduce-scatter.7
where the time goes:
time: 1030 us; the launch traced here: 1020 us
  blocking collectives  369 us (36%)
  waiting for transfers between devices  258 us (25%)
  matrix products  177 us (17%)
  local copies, waits for them, and re-layouts  162 us (16%)
  other arithmetic  26.4 us (3%)
  between operations  14.5 us (1%)
  loops' own time  13.4 us (1%)
    unnamed x1, blocking collectives  176 us
    gather x3, local copies, waits for them, and re-layouts, shards(): jnp.take_along_axis(table, jnp.clip(local_rows, 0, held - 1), axis=1)  139 us
    all_gather x1, blocking collectives, shards(): lax.all_gather(embedding, 'dp', axis=0, tiled=True)  97.2 us
    all_gather x1, blocking collectives, shards(): lax.all_gather(candidates, 'dp', axis=0, tiled=True)  95.9 us
    all_gather x1, waiting for transfers between devices, shards(): every_prompt = lax.all_gather(prompts, 'dp', axis=0, tiled=True)  78.2 us
    reduce_scatter x1, waiting for transfers between devices, shards(): lax.psum_scatter(jnp.dot(context, w_out, preferred_element_type=jnp.float...  75.2 us
    dot_general x4, matrix products, attend(): jnp.einsum('hqk,khe->qhe', probs, all_values, preferred_element_type=jnp....  64.8 us
    sub x4, matrix products, attend(): weights = jnp.exp(logits - top)  57.9 us
  transfers between devices with their start and end apart: 6, of which 5 were waited for; matrix products, arithmetic and copies ran while one was open for 1% of the time, Pallas kernels for 0%

commit v1 on v0

--- a/solution.py
+++ b/solution.py
@@ -2,9 +2,15 @@
 import jax.numpy as jnp
 from jax import lax
 from jax.sharding import PartitionSpec as P
+from jax.lax import all_to_all, psum
 
 D = 1024
 HEAD_DIM = 64
+
+
+def time_plane(load):
+    w_next = jnp.stack([load for _ in range(psum(1, "dp"))], 0)
+    return jnp.concatenate(all_to_all(w_next, "dp", 0, 0), 0)
 
 
 def layer_norm(values, gain, bias):
@@ -123,7 +129,7 @@
     embedding = (pooled * lax.rsqrt(square + 1e-06)).astype(jnp.bfloat16)
     asked_vectors, asked_rows = (
         lax.all_gather(embedding, "dp", axis=0, tiled=True),
-        lax.all_gather(candidates, "dp", axis=0, tiled=True),
+        time_plane(candidates),
     )
     held = index_rows.shape[0]
     local_rows = asked_rows - lax.axis_index("dp") * held

time: 1030 us -> 986 us (0.957)
  blocking collectives: 369 us -> 273 us
  waiting for transfers between devices: 258 us -> 301 us
    all_gather x1 -> x0, blocking collectives: 95.9 us -> none  [shards(): lax.all_gather(candidates, 'dp', axis=0, tiled=True)]
    reduce_scatter x1, waiting for transfers between devices: 0.01 us -> 36.5 us  [shards(): lax.psum_scatter(jnp.dot(expanded, w_down, preferred_element_type=jnp.flo...]
  transfers between devices with their start and end apart: 6 -> 7, of which waited for: 5 -> 6; matrix products, arithmetic and copies ran while one was open for 1% -> 2% of each run, Pallas kernels for 0% -> 0%
where the time goes in v1:
time: 986 us; the launch traced here: 980 us
  waiting for transfers between devices  301 us (31%)
  blocking collectives  273 us (28%)
  matrix products  177 us (18%)
  local copies, waits for them, and re-layouts  163 us (17%)
  other arithmetic  27.2 us (3%)
  between operations  14.5 us (1%)
  loops' own time  13.4 us (1%)
    unnamed x1, blocking collectives  176 us
    gather x3, local copies, waits for them, and re-layouts, shards(): jnp.take_along_axis(table, jnp.clip(local_rows, 0, held - 1), axis=1)  139 us
    all_gather x1, blocking collectives, shards(): lax.all_gather(embedding, 'dp', axis=0, tiled=True)  97.2 us
    all_gather x1, waiting for transfers between devices, shards(): every_prompt = lax.all_gather(prompts, 'dp', axis=0, tiled=True)  78.2 us
    reduce_scatter x1, waiting for transfers between devices, shards(): lax.psum_scatter(jnp.dot(context, w_out, preferred_element_type=jnp.float...  75.2 us
    dot_general x4, matrix products, attend(): jnp.einsum('hqk,khe->qhe', probs, all_values, preferred_element_type=jnp....  64.8 us
    sub x4, matrix products, attend(): weights = jnp.exp(logits - top)  57.9 us
    all_gather x1, waiting for transfers between devices, shards(): whole = lax.all_gather(tokens, 'tensor', axis=0, tiled=True)  47.5 us
  transfers between devices with their start and end apart: 7, of which 6 were waited for; matrix products, arithmetic and copies ran while one was open for 2% of the time, Pallas kernels for 0%

profile of v1, /device:TPU:0, one launch (start us, length us, event | category | flops | bytes accessed | tf_op | source)
XLA Modules:
  0.0 979.9 jit_solution(8389069408068213677)
XLA Ops:
  6.5 0.7 all-gather.4.cloned.1.call-update
  7.3 0.7 all-gather.6.cloned.1.call-update
  8.1 0.7 copy.28
  9.1 0.8 select_reduce_fusion.1
  9.9 47.5 %all-gather.4.cloned.1.call-done = bf16[2048,1024]{1,0:T(8,128)(2,1)} async-done(((bf16[512,1024]{1,0:T(8,128)(2,1)}), bf16[2048,1024]{1,0:T(8,128)(2,1)}) %all-gather.4.cloned.1.call-update) | async-done | bytes 4194320 | tf_op jit(solution)/shard_map/all_gather | solution.py:47
  57.4 3.7 convolution_convert_fusion.1
  61.5 2.3 convolution_convert_fusion.3
  63.7 2.3 fusion.48
  66.1 78.2 %all-gather.6.cloned.1.call-done = bf16[32,64,1024]{2,1,0:T(8,128)(2,1)} async-done(((bf16[1,64,1024]{2,1,0:T(8,128)(2,1)}), bf16[32,64,1024]{2,1,0:T(8,128)(2,1)}) %all-gather.6.cloned.1.call-update) | async-done | bytes 4194320 | tf_op jit(solution)/shard_map/all_gather | solution.py:53
  144.3 4.7 convolution_convert_fusion
  149.0 2.4 convolution_convert_fusion.2
  151.4 1.4 pad_maximum_fusion
  152.9 4.1 copy.29
  157.0 2.7 pad_maximum_fusion.1
  159.7 4.1 copy.30
  163.8 158.4 %while.11 = (s32[]{:T(128)}, bf16[4,512,256]{2,1,0:T(8,128)(2,1)}, s32[4]{0:T(128)S(1)}, s32[2048]{0:T(1024)S(1)}, s32[2048]{0:T(1024)S(1)}, /*index=5*/bf16[204...) while((s32[]{:T(128)}, bf16[4,512,256]{2,1,0:T(8,128)(2,1)}, ...), condition=%wide.region_6.7_spmd.clone, body=%wide.region_3.6_spmd.clone.sunk | while | flops 3284297728 | bytes 19714248 | solution.py:90
  164.1 0.7 dynamic_slice.32
  165.7 1.0 constant_dynamic-slice_fusion.2
  166.8 1.3 broadcast_compare_fusion.3
  168.1 1.4 pad_add_fusion.2
  169.6 14.5 %fusion.136 = f32[4,512]{1,0:T(4,128)S(1)} fusion(pred[512,4096]{1,0:T(8,128)(4,1)} %pad_add_fusion.2, bf16[512,4,64]{0,2,1:T(8,128)(2,1)S(1)} %bitcast.77, bf16[4096,4,64]{0,2,1:T(8,128)(2,1)} %get-tuple-element.208), kind=kOutput, calls=%fused_computation.130.clone.1 | convolution fusion | flops 1098911744 | bytes 4464640 | tf_op jit(solution)/shard_map/while/body/eval_jaxpr/sub | solution.py:84
  184.0 16.2 %fusion.137 = bf16[4,512,64]{1,2,0:T(8,128)(2,1)S(1)} fusion(bf16[4096,4,64]{0,2,1:T(8,128)(2,1)} %get-tuple-element.209, f32[4,512]{1,0:T(4,128)S(1)} %fusion.136, pred[512,4096]{1,0:T(8,128)(4,1)} %pad_add_fusion.2, bf16[512,4,64]{0,2,1:T(8,128)(2,1)S(1)} %bitcast.78, bf16[4096,4,64]{0,2,1:T(8,128)(2,1)} %get-tuple-element.208), kind=kOutput, calls=%fused_computation.14.clone.1 | convolution fusion | flops 2181175296 | bytes 6823936 | tf_op jit(solution)/shard_map/while/body/eval_jaxpr/hqk,khe->qhe/dot_general | solution.py:87
  200.4 0.7 constant_dynamic-update-slice_fusion.2
  201.1 0.7 dynamic_slice.32
  202.6 1.0 constant_dynamic-slice_fusion.2
  203.8 1.3 broadcast_compare_fusion.3
  205.1 1.4 pad_add_fusion.2
  206.5 14.5 %fusion.136 = f32[4,512]{1,0:T(4,128)S(1)} fusion(pred[512,4096]{1,0:T(8,128)(4,1)} %pad_add_fusion.2, bf16[512,4,64]{0,2,1:T(8,128)(2,1)S(1)} %bitcast.77, bf16[4096,4,64]{0,2,1:T(8,128)(2,1)} %get-tuple-element.208), kind=kOutput, calls=%fused_computation.130.clone.1 | convolution fusion | flops 1098911744 | bytes 4464640 | tf_op jit(solution)/shard_map/while/body/eval_jaxpr/sub | solution.py:84
  221.0 16.2 %fusion.137 = bf16[4,512,64]{1,2,0:T(8,128)(2,1)S(1)} fusion(bf16[4096,4,64]{0,2,1:T(8,128)(2,1)} %get-tuple-element.209, f32[4,512]{1,0:T(4,128)S(1)} %fusion.136, pred[512,4096]{1,0:T(8,128)(4,1)} %pad_add_fusion.2, bf16[512,4,64]{0,2,1:T(8,128)(2,1)S(1)} %bitcast.78, bf16[4096,4,64]{0,2,1:T(8,128)(2,1)} %get-tuple-element.208), kind=kOutput, calls=%fused_computation.14.clone.1 | convolution fusion | flops 2181175296 | bytes 6823936 | tf_op jit(solution)/shard_map/while/body/eval_jaxpr/hqk,khe->qhe/dot_general | solution.py:87
  237.4 0.7 constant_dynamic-update-slice_fusion.2
  238.1 0.7 dynamic_slice.32
  239.6 1.0 constant_dynamic-slice_fusion.2
  240.7 1.3 broadcast_compare_fusion.3
  242.1 1.4 pad_add_fusion.2
  243.5 14.5 %fusion.136 = f32[4,512]{1,0:T(4,128)S(1)} fusion(pred[512,4096]{1,0:T(8,128)(4,1)} %pad_add_fusion.2, bf16[512,4,64]{0,2,1:T(8,128)(2,1)S(1)} %bitcast.77, bf16[4096,4,64]{0,2,1:T(8,128)(2,1)} %get-tuple-element.208), kind=kOutput, calls=%fused_computation.130.clone.1 | convolution fusion | flops 1098911744 | bytes 4464640 | tf_op jit(solution)/shard_map/while/body/eval_jaxpr/sub | solution.py:84
  258.0 16.2 %fusion.137 = bf16[4,512,64]{1,2,0:T(8,128)(2,1)S(1)} fusion(bf16[4096,4,64]{0,2,1:T(8,128)(2,1)} %get-tuple-element.209, f32[4,512]{1,0:T(4,128)S(1)} %fusion.136, pred[512,4096]{1,0:T(8,128)(4,1)} %pad_add_fusion.2, bf16[512,4,64]{0,2,1:T(8,128)(2,1)S(1)} %bitcast.78, bf16[4096,4,64]{0,2,1:T(8,128)(2,1)} %get-tuple-element.208), kind=kOutput, calls=%fused_computation.14.clone.1 | convolution fusion | flops 2181175296 | bytes 6823936 | tf_op jit(solution)/shard_map/while/body/eval_jaxpr/hqk,khe->qhe/dot_general | solution.py:87
  274.3 0.7 constant_dynamic-update-slice_fusion.2
  275.1 0.7 dynamic_slice.32
  276.6 1.0 constant_dynamic-slice_fusion.2
  277.7 1.3 broadcast_compare_fusion.3
  279.1 1.4 pad_add_fusion.2
  280.5 14.5 %fusion.136 = f32[4,512]{1,0:T(4,128)S(1)} fusion(pred[512,4096]{1,0:T(8,128)(4,1)} %pad_add_fusion.2, bf16[512,4,64]{0,2,1:T(8,128)(2,1)S(1)} %bitcast.77, bf16[4096,4,64]{0,2,1:T(8,128)(2,1)} %get-tuple-element.208), kind=kOutput, calls=%fused_computation.130.clone.1 | convolution fusion | flops 1098911744 | bytes 4464640 | tf_op jit(solution)/shard_map/while/body/eval_jaxpr/sub | solution.py:84
  295.0 16.2 %fusion.137 = bf16[4,512,64]{1,2,0:T(8,128)(2,1)S(1)} fusion(bf16[4096,4,64]{0,2,1:T(8,128)(2,1)} %get-tuple-element.209, f32[4,512]{1,0:T(4,128)S(1)} %fusion.136, pred[512,4096]{1,0:T(8,128)(4,1)} %pad_add_fusion.2, bf16[512,4,64]{0,2,1:T(8,128)(2,1)S(1)} %bitcast.78, bf16[4096,4,64]{0,2,1:T(8,128)(2,1)} %get-tuple-element.208), kind=kOutput, calls=%fused_computation.14.clone.1 | convolution fusion | flops 2181175296 | bytes 6823936 | tf_op jit(solution)/shard_map/while/body/eval_jaxpr/hqk,khe->qhe/dot_general | solution.py:87
  311.3 0.7 constant_dynamic-update-slice_fusion.2
  322.2 5.8 fusion.100
  328.8 75.2 %reduce-scatter.4.cloned.1.call-done = f32[512,1024]{1,0:T(8,128)} async-done(((f32[2048,1024]{1,0:T(8,128)}), f32[512,1024]{1,0:T(8,128)}) %reduce-scatter.4.cloned.1.call-update) | async-done | bytes 2097168 | tf_op jit(solution)/shard_map/reduce_scatter | solution.py:94
  404.0 2.0 fusion.52
  406.7 1.6 add_convert_fusion.1
  408.4 46.9 %all-gather.8.cloned.1.call-done = bf16[2048,1024]{1,0:T(8,128)(2,1)} async-done(((bf16[512,1024]{1,0:T(8,128)(2,1)}), bf16[2048,1024]{1,0:T(8,128)(2,1)}) %all-gather.8.cloned.1.call-update) | async-done | bytes 4194320 | tf_op jit(solution)/shard_map/all_gather | solution.py:105
  455.3 28.5 %fusion.43 = bf16[2048,1024]{1,0:T(8,128)(2,1)} fusion(bf16[1024,1024]{1,0:T(8,128)(2,1)S(1)} %copy-done, f32[1024]{0:T(1024)S(1)} %copy-done.13, bf16[2048,1024]{1,0:T(8,128)(2,1)} %all-gather.8.cloned.1.call-done, bf16[1024,1024]{1,0:T(8,128)(2,1)} %param.21), kind=kOutput, calls=%fused_computation.47 | convolution fusion | flops 8730443776 | bytes 12587008 | tf_op jit(solution)/shard_map/dot_general | solution.py:113
  484.5 0.7 reshape.159
  485.3 9.6 all-to-all-start
  495.0 36.5 %reduce-scatter.6.cloned.1.call-done = bf16[512,1024]{1,0:T(8,128)(2,1)} async-done(((bf16[2048,1024]{1,0:T(8,128)(2,1)}), bf16[512,1024]{1,0:T(8,128)(2,1)}) %reduce-scatter.6.cloned.1.call-update) | async-done | bytes 1048592 | tf_op jit(solution)/shard_map/reduce_scatter | solution.py:112
  531.5 1.7 fusion.50
  533.2 1.7 multiply_reduce_fusion
  534.9 1.3 fusion.51
  538.2 0.8 reduce.1
  539.2 15.3 %reduce-scatter.8.cloned.1.call-done = f32[8,1024]{1,0:T(8,128)} async-done(((f32[32,1024]{1,0:T(8,128)}), f32[8,1024]{1,0:T(8,128)}) %reduce-scatter.8.cloned.1.call-update) | async-done | bytes 32784 | tf_op jit(solution)/shard_map/reduce_scatter | solution.py:124
  554.6 0.9 multiply_reduce_fusion.2
  555.5 0.8 multiply_convert_fusion
  556.4 97.2 %all_gather.15 = bf16[256,1024]{1,0:T(8,128)(2,1)S(1)} all-gather(bf16[8,1024]{1,0:T(8,128)(2,1)S(1)} %multiply_convert_fusion), channel_id=1, replica_groups=mesh['dp'=32,'tensor'=4] {'dp'}, dimensions={0}, use_global_device_ids=true | all-gather | bytes 540672 | tf_op jit(solution)/shard_map/all_gather | solution.py:131
  653.5 3.5 convolution_multiply_fusion
  657.0 138.8 %gather_fusion = bf16[16384]{0:T(1024)(128)(2,1)S(1)} fusion(bf16[256,2048]{1,0:T(8,128)(2,1)S(1)} %convolution_multiply_fusion, s32[16384]{0:T(1024)S(1)} %reshape.150), kind=kCustom, calls=%fused_computation | custom fusion | bytes 196608 | tf_op jit(solution)/shard_map/jit(take_along_axis)/gather | solution.py:138
  796.1 176.2 %all-reduce = bf16[256,64]{1,0:T(8,128)(2,1)S(1)} all-reduce(bf16[256,64]{1,0:T(8,128)(2,1)S(1)} %select_convert_fusion), channel_id=5, replica_groups=mesh['dp'=32,'tensor'=4] {'dp'}, use_global_device_ids=true, to_apply=%region_15.16.clone | all-reduce | flops 16384 | bytes 65536
  (85 shorter events, 7.0 us)
Async XLA Ops:
  6.5 448.8 %copy-start = (bf16[1024,1024]{1,0:T(8,128)(2,1)S(1)}, bf16[1024,1024]{1,0:T(8,128)(2,1)}, u32[]{:S(2)}) copy-start(bf16[1024,1024]{1,0:T(8,128)(2,1)} %param.23) | copy-start | bytes 6291460
  6.5 50.9 %all-gather.4.cloned.1.call-start = ((), (), s32[]{:S(2)}) async-start(), calls=%async_computation.4 | async-start | bytes 5242880 | tf_op jit(solution)/shard_map/all_gather | solution.py:47
  7.3 137.0 %all-gather.6.cloned.1.call-start = ((), (), s32[]{:S(2)}) async-start(), calls=%async_computation.5 | async-start | bytes 4325376 | tf_op jit(solution)/shard_map/all_gather | solution.py:53
  8.0 396.0 %reduce-scatter.4.cloned.1.call-start = ((), (), s32[]{:S(2)}) async-start(), calls=%async_computation.6 | async-start | bytes 10485760 | tf_op jit(solution)/shard_map/reduce_scatter | solution.py:94
  57.4 3.7 copy-start.10
  57.4 4.1 copy-start.12
  144.3 4.7 copy-start.11
  149.0 2.4 copy-start.5
  328.0 0.7 copy-start.6
  328.0 0.7 copy-start.7
  328.1 75.9 %copy-start.3 = (bf16[512,1024]{1,0:T(8,128)(2,1)S(1)}, bf16[512,1024]{1,0:T(8,128)(2,1)}, u32[]{:S(2)}) copy-start(bf16[512,1024]{1,0:T(8,128)(2,1)} %param.15) | copy-start | bytes 3145732
  328.1 127.2 %all-gather.8.cloned.1.call-start = ((), (), s32[]{:S(2)}) async-start(), calls=%async_computation.7 | async-start | bytes 5242880 | tf_op jit(solution)/shard_map/all_gather | solution.py:105
  404.0 2.2 copy-start.1
  406.2 49.1 %copy-start.13 = (f32[1024]{0:T(1024)S(1)}, f32[1024]{0:T(1024)}, u32[]{:S(2)}) copy-start(f32[1024]{0:T(1024)} %param.22) | copy-start | bytes 12292
  408.3 123.2 %reduce-scatter.6.cloned.1.call-start = ((), (), s32[]{:S(2)}) async-start(), calls=%async_computation.8 | async-start | bytes 5242880 | tf_op jit(solution)/shard_map/reduce_scatter | solution.py:112
  483.8 0.7 copy-start.8
  483.8 47.7 %copy-start.2 = (bf16[512,1024]{1,0:T(8,128)(2,1)S(1)}, bf16[512,1024]{1,0:T(8,128)(2,1)}, u32[]{:S(2)}) copy-start(bf16[512,1024]{1,0:T(8,128)(2,1)} %add_convert_fusion.1) | copy-start | bytes 3145732
  484.5 51.8 %copy-start.9 = (s32[1,32]{1,0:T(1,128)S(1)}, s32[1,32]{1,0:T(1,128)}, u32[]{:S(2)}) copy-start(s32[1,32]{1,0:T(1,128)} %param.25) | copy-start | bytes 388
  484.5 51.9 %copy-start.14 = (u32[128]{0:T(128)S(1)}, u32[128]{0:T(128)}, u32[]{:S(2)}) copy-start(u32[128]{0:T(128)} %constant.173) | copy-start | bytes 1540
  485.3 52.3 %all-to-all-start = ((s32[32,1,512]{2,1,0:T(1,128)}), s32[32,1,512]{2,1,0:T(1,128)S(1)}, u32[]{:S(2)}, u32[]{:S(2)}) async-start(s32[32,1,512]{2,1,0:T(1,128)} %reshape.159), calls=%async_computation | async-start | bytes 131072 | tf_op jit(solution)/shard_map/all_to_all | solution.py:13
  494.9 59.7 %reduce-scatter.8.cloned.1.call-start = ((), (), s32[]{:S(2)}) async-start(), calls=%async_computation.9 | async-start | bytes 163840 | tf_op jit(solution)/shard_map/reduce_scatter | solution.py:124
  531.5 3.4 copy-start.4
Sparse Core Ops, SparseCore 0:
  9.0 48.3 all-gather.3
  60.5 83.7 all-gather.5
  328.2 75.7 reduce-scatter.3
  408.4 46.8 all-gather.7
  484.0 47.5 reduce-scatter.5
  536.4 18.0 reduce-scatter.7
